TPU v7x, 256 devices: a whole 4x4x8 slice. The times are simulated.
256 devices in a mesh: ctx: 32 (over z, y_hi, core), mp: 8 (over x, y_lo).
Axes of the slice: x: 4, y: 4 (y_hi: 2, y_lo: 2; y = y_hi * 2 + y_lo), z: 8, core: 2. Of those that a mesh axis runs over, the one named last changes fastest.
Arguments:
- proj: bfloat16 [8192, 3, 8192], P(('ctx', 'mp')), may hold values from -6 to 6
- conv_weight: float32 [3, 7, 8192], replicated, may hold values from -2 to 2
- residues: float32 [128, 16], P('mp'), may hold values from -1.5 to 1.5
- decays: float32 [128, 16], P('mp'), may hold values from 1.2207031e-05 to 0.03
- doc_lengths: int32 [64], replicated, may hold values from 1 to 768, 8192 in all
Outputs:
- mixed: bfloat16 [8192, 8192], P(('ctx', 'mp'))
All inputs are finite; a program needn't handle non-finite values.
Results may differ from a plain program's by a relative error of at most 0.014.
Values may be sent and summed in bfloat16 or wider, within the bound.
No kernel may reach another device: no remote copies, remote signals or barrier semaphores. Data moves between devices by JAX's collectives and lax.ppermute only.
A program may use at most 64 MiB of HBM per device.

v0:
```python
import jax
import jax.numpy as jnp
from jax import lax
from jax.sharding import PartitionSpec as P


def shifted_2(block, axis, distance):
    devices = range(lax.axis_size(axis))
    route = [(i - distance, i) for i in devices if i - distance in devices]
    return lax.ppermute(block, axis, route)


def document_number_index(doc_lengths, positions):
    doc_starts = jnp.cumsum(doc_lengths) - doc_lengths
    inside = (doc_starts[None, :] <= positions[:, None]).astype(jnp.int32)
    return jnp.sum(inside, axis=1) - 1


def short_convolution(padded, conv_weight, padded_document_ids, padded_pos, out_rows):
    kernel_len = conv_weight.shape[1]
    result = jnp.zeros((out_rows,) + padded.shape[1:], jnp.float32)
    own_docs = padded_document_ids[kernel_len - 1 :]
    for position_shift in range(kernel_len):
        begin_row = kernel_len - 1 - position_shift
        earlier = padded[begin_row : begin_row + out_rows].astype(jnp.float32)
        keep_mask = (padded_document_ids[begin_row : begin_row + out_rows] == own_docs) & (
            padded_pos[begin_row : begin_row + out_rows] >= 0
        )
        result = (
            result
            + conv_weight[:, position_shift, :][None]
            * earlier
            * keep_mask.astype(jnp.float32)[:, None, None]
        )
    return result


def filter_tile(coefficient, decays, out_index, piece_start, width_in):
    span = float(width_in)
    out_float = (out_index - piece_start).astype(jnp.float32)
    shifted = jnp.maximum(out_float - span, -span)
    left_neighbor = coefficient[:, :, None] * jnp.exp(-decays[:, :, None] * shifted[None, None, :])
    in_offsets = jnp.arange(width_in).astype(jnp.float32)
    right_neighbor = jnp.exp(-decays[:, :, None] * (span - in_offsets)[None, None, :])
    token_tile_rows = jnp.einsum(
        "ejz,ejx->ezx", left_neighbor, right_neighbor, precision=lax.Precision.HIGHEST
    )
    lag_matrix = (out_index - piece_start)[:, None] - jnp.arange(width_in, dtype=jnp.int32)[None, :]
    return jnp.where((lag_matrix >= 0)[None], token_tile_rows, 0.0)


def split_product(form, weights, inputs):
    upper_part = weights.astype(jnp.bfloat16)
    lower_part = (weights - upper_part.astype(jnp.float32)).astype(jnp.bfloat16)
    first = jnp.einsum(form, upper_part, inputs, preferred_element_type=jnp.float32)
    return first + jnp.einsum(form, lower_part, inputs, preferred_element_type=jnp.float32)


def long_filter(product, residues, decays, block_begin_position):
    block_len = product.shape[0]
    channels = product.shape[1]
    group_count = residues.shape[0]
    group_width = channels // group_count
    coefficient = residues * jnp.sqrt(decays)
    out_index = block_begin_position + jnp.arange(block_len, dtype=jnp.int32)

    def one_tile(running, rows_part, part_start):
        width_in = rows_part.shape[0]
        token_tile_rows = filter_tile(coefficient, decays, out_index, part_start, width_in)
        inputs = rows_part.reshape(width_in, group_count, group_width)
        return running + split_product("grs,sgc->rgc", token_tile_rows, inputs)

    initial = jnp.zeros((block_len, group_count, group_width), jnp.float32)
    piece_rows = lax.all_gather(product, "ctx", axis=0, tiled=True)
    width_in = piece_rows.shape[0]
    count_blocks = width_in // block_len
    stacked = piece_rows.reshape(count_blocks, block_len, channels)
    starts = block_len * jnp.arange(count_blocks, dtype=jnp.int32)

    def scan_step(carry, pair):
        return (one_tile(carry, pair[0], pair[1]), None)

    result, unused = lax.scan(scan_step, initial, (stacked, starts))
    return result.reshape(block_len, channels).astype(jnp.bfloat16)


def shards(proj, conv_weight, residues, decays, doc_lengths):
    kernel_len = conv_weight.shape[1]
    channel_rows = lax.all_to_all(proj, "mp", split_axis=2, concat_axis=0, tiled=True)
    block_len = channel_rows.shape[0]
    channels = channel_rows.shape[2]
    local_weight = lax.dynamic_slice_in_dim(
        conv_weight, lax.axis_index("mp") * channels, channels, 2
    )
    tail_rows = shifted_2(channel_rows[block_len - (kernel_len - 1) :], "ctx", 1)
    block_begin_position = lax.axis_index("ctx") * block_len
    padded_pos = (
        block_begin_position
        - (kernel_len - 1)
        + jnp.arange(block_len + kernel_len - 1, dtype=jnp.int32)
    )
    padded_document_ids = document_number_index(doc_lengths, padded_pos)
    padded = jnp.concatenate([tail_rows, channel_rows], axis=0)
    conv = short_convolution(padded, local_weight, padded_document_ids, padded_pos, block_len)
    query_part = conv[:, 0]
    product = (conv[:, 1] * conv[:, 2]).astype(jnp.bfloat16)
    filtered = long_filter(product, residues, decays, block_begin_position)
    mixed_out = (query_part * filtered.astype(jnp.float32)).astype(jnp.bfloat16)
    return lax.all_to_all(mixed_out, "mp", split_axis=0, concat_axis=1, tiled=True)


def solution(mesh):
    return jax.shard_map(
        shards,
        mesh=mesh,
        in_specs=(P(("ctx", "mp"), None, None), P(), P("mp", None), P("mp", None), P()),
        out_specs=P(("ctx", "mp"), None),
        check_vma=False,
    )
```

profile of v0, /device:TPU:8, one launch (start us, length us, event | category | flops | bytes accessed | tf_op | source)
XLA Modules:
  0.0 531.1 jit_solution(9122464082286298592)
XLA Ops:
  6.5 10.6 %copy.23 = bf16[32,3,8192]{0,1,2:T(4,128)(2,1)} copy(bf16[32,3,8192]{2,0,1:T(8,128)(2,1)} %param.7) | data formatting | bytes 3145728 | tf_op args[0]
  17.2 9.8 %reshape.117 = bf16[8,2,49152]{2,1,0:T(2,128)(2,1)} reshape(bf16[8192,3,32]{2,1,0:T(4,128)(2,1)} %bitcast.54) | data formatting | bytes 3145728
  27.0 5.9 %all-to-all-start = ((bf16[8,2,49152]{2,1,0:T(2,128)(2,1)}), bf16[8,2,49152]{2,1,0:T(2,128)(2,1)S(1)}, u32[]{:S(2)}, u32[]{:S(2)}) async-start(bf16[8,2,49152]{2,1,0:T(2,128)(2,1)} %reshape.117), calls=%async_computation | async-start | bytes 3145728 | tf_op jit(solution)/shard_map/all_to_all | solution.py:89
  35.0 19.6 %all-to-all-done = bf16[8,2,49152]{2,1,0:T(2,128)(2,1)S(1)} async-done(((bf16[8,2,49152]{2,1,0:T(2,128)(2,1)}), bf16[8,2,49152]{2,1,0:T(2,128)(2,1)S(1)}, u32[]{:S(2)}, u32[]{:S(2)}) %all-to-all-start) | async-done | bytes 1572896 | tf_op jit(solution)/shard_map/all_to_all | solution.py:89
  54.7 7.6 %reshape.118 = bf16[8192,3,32]{2,1,0:T(4,128)(2,1)} reshape(bf16[8,2,49152]{2,1,0:T(2,128)(2,1)S(1)} %all-to-all-done) | data formatting | bytes 3145728
  62.3 10.5 %copy.31 = bf16[32,3,8,1024]{3,0,2,1:T(8,128)(2,1)S(1)} copy(bf16[32,3,8,1024]{0,1,3,2:T(4,128)(2,1)} %bitcast.53) | data formatting | bytes 3145728 | tf_op jit(solution)/shard_map/all_to_all | solution.py:89
  75.0 3.9 multiply_add_fusion
  80.4 142.8 %all-gather.3.cloned.1.call-done = bf16[8192,1,1024]{2,0,1:T(8,128)(2,1)} async-done(((bf16[256,1,1024]{2,0,1:T(8,128)(2,1)}), bf16[8192,1,1024]{2,0,1:T(8,128)(2,1)}) %all-gather.3.cloned.1.call-update) | async-done | bytes 16777232 | tf_op jit(solution)/shard_map/all_gather | solution.py:74
  223.1 282.1 %while.13 = (s32[]{:T(128)}, f32[256,16,64]{0,2,1:T(8,128)S(1)}, bf16[32,256,1024]{2,1,0:T(8,128)(2,1)}, s32[32]{0:T(128)S(1)}, f32[16,16]{1,0:T(8,128)S(1)}, /*...) while((s32[]{:T(128)}, f32[256,16,64]{0,2,1:T(8,128)S(1)}, ...), condition=%wide.region_3.4_spmd.clone, body=%wide.region_2.3_spmd.clone.sunk | while | flops 477169920 | bytes 20127888 | solution.py:83
  226.4 3.7 fusion.42
  235.3 3.7 fusion.42
  270.5 3.7 fusion.42
  279.3 3.7 fusion.42
  288.2 3.7 fusion.42
  297.0 3.7 fusion.42
  305.8 3.7 fusion.42
  314.6 3.7 fusion.42
  358.7 3.7 fusion.42
  367.5 3.7 fusion.42
  376.3 3.7 fusion.42
  385.1 3.7 fusion.42
  394.0 3.7 fusion.42
  402.8 3.7 fusion.42
  508.6 14.8 %all_to_all.34 = bf16[8,32,1024]{2,1,0:T(8,128)(2,1)S(1)} all-to-all(bf16[8,32,1024]{2,1,0:T(8,128)(2,1)S(1)} %multiply_convert_fusion), channel_id=1, replica_groups=mesh['ctx'=32,'mp'=8] {'mp'}, dimensions={0} | all-to-all | bytes 1048576 | tf_op jit(solution)/shard_map/all_to_all | solution.py:109
  (308 shorter events, 237.5 us)
Async XLA Ops:
  27.0 5.9 %copy-start.2 = (s32[64]{0:T(128)S(1)}, s32[64]{0:T(128)}, u32[]{:S(2)}) copy-start(s32[64]{0:T(128)} %param.11) | copy-start | bytes 772
  27.0 27.7 %all-to-all-start = ((bf16[8,2,49152]{2,1,0:T(2,128)(2,1)}), bf16[8,2,49152]{2,1,0:T(2,128)(2,1)S(1)}, u32[]{:S(2)}, u32[]{:S(2)}) async-start(bf16[8,2,49152]{2,1,0:T(2,128)(2,1)} %reshape.117), calls=%async_computation | async-start | bytes 3145728 | tf_op jit(solution)/shard_map/all_to_all | solution.py:89
  32.8 190.3 %all-gather.3.cloned.1.call-start = ((), (), s32[]{:S(2)}) async-start(), calls=%async_computation.2 | async-start | bytes 17301504 | tf_op jit(solution)/shard_map/all_gather | solution.py:74
  72.8 2.2 collective-permute-start
  78.9 1.4 copy-start
  78.9 1.4 copy-start.1
Sparse Core Ops, SparseCore 0:
  80.4 142.6 all-gather.2
where the time goes:
time: 534 us; the launch traced here: 531 us
  matrix products  175 us (33%)
  waiting for transfers between devices  163 us (31%)
  local copies, waits for them, and re-layouts  103 us (19%)
  other arithmetic  52.4 us (10%)
  blocking collectives  14.8 us (3%)
  between operations  13.6 us (3%)
  starting transfers between devices  7.36 us (1%)
    all_gather x1, waiting for transfers between devices, long_filter(): piece_rows = lax.all_gather(product, 'ctx', axis=0, tiled=True)  143 us
    dot_general x32, matrix products, filter_tile(): jnp.einsum('ejz,ejx->ezx', left_neighbor, right_neighbor, precision=lax.P...  119 us
    dynamic_slice x96, local copies, waits for them, and re-layouts, long_filter(): result, unused = lax.scan(scan_step, initial, (stacked, starts))  59.9 us
    dot_general x32, matrix products, split_product(): jnp.einsum(form, lower_part, inputs, preferred_element_type=jnp.float32)  31.6 us
    unnamed x13, local copies, waits for them, and re-layouts  28.1 us
    dot_general x32, matrix products, split_product(): jnp.einsum(form, upper_part, inputs, preferred_element_type=jnp.float32)  23.8 us
    sub x32, other arithmetic, filter_tile(): span - in_offsets  20.9 us
    sub x32, other arithmetic, filter_tile(): out_index - piece_start  20.7 us
  transfers between devices with their start and end apart: 3, of which 3 were waited for; matrix products, arithmetic and copies ran while one was open for 0% of the time, Pallas kernels for 0%

commit v1 on v0

--- a/solution.py
+++ b/solution.py
@@ -86,7 +86,15 @@
 
 def shards(proj, conv_weight, residues, decays, doc_lengths):
     kernel_len = conv_weight.shape[1]
-    channel_rows = lax.all_to_all(proj, "mp", split_axis=2, concat_axis=0, tiled=True)
+    channel_rows = jnp.concatenate(
+        jax.lax.all_to_all(
+            jnp.stack(jnp.split(proj, jax.lax.psum(1, "mp"), axis=2)),
+            "mp",
+            split_axis=0,
+            concat_axis=0,
+        ),
+        axis=0,
+    )
     block_len = channel_rows.shape[0]
     channels = channel_rows.shape[2]
     local_weight = lax.dynamic_slice_in_dim(

time: 534 us -> 508 us (0.951)
  local copies, waits for them, and re-layouts: 103 us -> 77.5 us
    unnamed x13 -> x17, local copies, waits for them, and re-layouts: 28.1 us -> 11.4 us
    all_to_all x1, local copies, waits for them, and re-layouts: 10.5 us -> 0.18 us  [shards(): jax.lax.all_to_all(jnp.stack(jnp.split(proj, jax.lax.psum(1, 'mp'), axis=...]
where the time goes in v1:
time: 508 us; the launch traced here: 506 us
  matrix products  175 us (34%)
  waiting for transfers between devices  163 us (32%)
  local copies, waits for them, and re-layouts  77.5 us (15%)
  other arithmetic  52.4 us (10%)
  blocking collectives  14.8 us (3%)
  between operations  13.6 us (3%)
  starting transfers between devices  7.05 us (1%)
    all_gather x1, waiting for transfers between devices, long_filter(): piece_rows = lax.all_gather(product, 'ctx', axis=0, tiled=True)  143 us
    dot_general x32, matrix products, filter_tile(): jnp.einsum('ejz,ejx->ezx', left_neighbor, right_neighbor, precision=lax.P...  119 us
    dynamic_slice x96, local copies, waits for them, and re-layouts, long_filter(): result, unused = lax.scan(scan_step, initial, (stacked, starts))  59.9 us
    dot_general x32, matrix products, split_product(): jnp.einsum(form, lower_part, inputs, preferred_element_type=jnp.float32)  31.6 us
    dot_general x32, matrix products, split_product(): jnp.einsum(form, upper_part, inputs, preferred_element_type=jnp.float32)  23.8 us
    sub x32, other arithmetic, filter_tile(): span - in_offsets  20.9 us
    sub x32, other arithmetic, filter_tile(): out_index - piece_start  20.7 us
    all_to_all x1, waiting for transfers between devices, shards(): jax.lax.all_to_all(jnp.stack(jnp.split(proj, jax.lax.psum(1, 'mp'), axis=...  19.6 us
  transfers between devices with their start and end apart: 3, of which 3 were waited for; matrix products, arithmetic and copies ran while one was open for 0% of the time, Pallas kernels for 0%

profile of v1, /device:TPU:8, one launch (start us, length us, event | category | flops | bytes accessed | tf_op | source)
XLA Modules:
  0.0 505.6 jit_solution(2499123381653605150)
XLA Ops:
  19.5 5.8 %all-to-all-start = ((bf16[8,32,3,1024]{3,1,2,0:T(8,128)(2,1)}), bf16[8,32,3,1024]{3,1,2,0:T(8,128)(2,1)S(1)}, u32[]{:S(2)}, u32[]{:S(2)}) async-start(bf16[8,32,3,1024]{3,1,2,0:T(8,128)(2,1)} %bitcast_dynamic-update-slice_fusion), calls=%async_computation | async-start | bytes 3145728 | tf_op jit(solution)/shard_map/all_to_all | solution.py:90
  27.4 19.6 %all-to-all-done = bf16[8,32,3,1024]{3,1,2,0:T(8,128)(2,1)S(1)} async-done(((bf16[8,32,3,1024]{3,1,2,0:T(8,128)(2,1)}), bf16[8,32,3,1024]{3,1,2,0:T(8,128)(2,1)S(1)}, u32[]{:S(2)}, u32[]{:S(2)}) %all-to-all-start) | async-done | bytes 1572896 | tf_op jit(solution)/shard_map/all_to_all | solution.py:90
  49.4 3.9 multiply_add_fusion
  54.8 142.8 %all-gather.3.cloned.1.call-done = bf16[8192,1,1024]{2,0,1:T(8,128)(2,1)} async-done(((bf16[256,1,1024]{2,0,1:T(8,128)(2,1)}), bf16[8192,1,1024]{2,0,1:T(8,128)(2,1)}) %all-gather.3.cloned.1.call-update) | async-done | bytes 16777232 | tf_op jit(solution)/shard_map/all_gather | solution.py:74
  197.6 282.1 %while.13 = (s32[]{:T(128)}, f32[256,16,64]{0,2,1:T(8,128)S(1)}, bf16[32,256,1024]{2,1,0:T(8,128)(2,1)}, s32[32]{0:T(128)S(1)}, f32[16,16]{1,0:T(8,128)S(1)}, /*...) while((s32[]{:T(128)}, f32[256,16,64]{0,2,1:T(8,128)S(1)}, ...), condition=%wide.region_3.4_spmd.clone, body=%wide.region_2.3_spmd.clone.sunk | while | flops 477169920 | bytes 20127888 | solution.py:83
  200.9 3.7 fusion.42
  209.7 3.7 fusion.42
  253.8 3.7 fusion.42
  262.6 3.7 fusion.42
  271.4 3.7 fusion.42
  280.2 3.7 fusion.42
  289.1 3.7 fusion.42
  297.9 3.7 fusion.42
  333.1 3.7 fusion.42
  342.0 3.7 fusion.42
  350.8 3.7 fusion.42
  359.6 3.7 fusion.42
  368.4 3.7 fusion.42
  377.2 3.7 fusion.42
  421.3 3.7 fusion.42
  430.1 3.7 fusion.42
  438.9 3.7 fusion.42
  447.8 3.7 fusion.42
  483.0 14.8 %all_to_all.21 = bf16[8,32,1024]{2,1,0:T(8,128)(2,1)S(1)} all-to-all(bf16[8,32,1024]{2,1,0:T(8,128)(2,1)S(1)} %multiply_convert_fusion), channel_id=1, replica_groups=mesh['ctx'=32,'mp'=8] {'mp'}, dimensions={0} | all-to-all | bytes 1048576 | tf_op jit(solution)/shard_map/all_to_all | solution.py:117
  (313 shorter events, 235.7 us)
Async XLA Ops:
  6.5 18.7 %copy-start.2 = (s32[64]{0:T(128)S(1)}, s32[64]{0:T(128)}, u32[]{:S(2)}) copy-start(s32[64]{0:T(128)} %param.11) | copy-start | bytes 772
  19.5 27.6 %all-to-all-start = ((bf16[8,32,3,1024]{3,1,2,0:T(8,128)(2,1)}), bf16[8,32,3,1024]{3,1,2,0:T(8,128)(2,1)S(1)}, u32[]{:S(2)}, u32[]{:S(2)}) async-start(bf16[8,32,3,1024]{3,1,2,0:T(8,128)(2,1)} %bitcast_dynamic-update-slice_fusion), calls=%async_computation | async-start | bytes 3145728 | tf_op jit(solution)/shard_map/all_to_all | solution.py:90
  25.2 172.4 %all-gather.3.cloned.1.call-start = ((), (), s32[]{:S(2)}) async-start(), calls=%async_computation.2 | async-start | bytes 17301504 | tf_op jit(solution)/shard_map/all_gather | solution.py:74
  47.3 2.2 collective-permute-start
  53.3 1.4 copy-start
  53.4 1.4 copy-start.1
Sparse Core Ops, SparseCore 0:
  54.9 142.6 all-gather.2
